TPU v7x, 32 devices: a whole 2x2x4 slice. The times are simulated.
32 devices in a mesh: clips: 2 (over y), tm: 4 (over x, core), rows: 4 (over z).
Axes of the slice: x: 2, y: 2, z: 4, core: 2. Of those that a mesh axis runs over, the one named last changes fastest.
Arguments:
- segment_input: bfloat16 [4, 8, 4, 32, 384], P('clips', 'tm', 'rows'), parts along dimension 0, may hold values from -6 to 6
- inner_input: bfloat16 [4, 8, 4, 32, 384], P('clips', 'tm', 'rows'), parts along dimension 0, may hold values from -6 to 6
- lengths: int32 [4, 4], P('clips', 'tm'), parts along dimension 0, may hold values from 1 to 2
- inner_gain: float32 [384], replicated, may hold values from 0.25 to 1.75
- causal_weight: bfloat16 [3, 3, 3, 384, 384], replicated, may hold values from -0.0625 to 0.0625
- causal_bias: float32 [384], replicated, may hold values from -3 to 3
- attention_gain: float32 [384], replicated, may hold values from 0.25 to 1.75
- triple_weight: bfloat16 [384, 1152], replicated, may hold values from -0.4375 to 0.4375
- triple_bias: float32 [1152], replicated, may hold values from -150 to 150
- output_weight: bfloat16 [384, 384], replicated, may hold values from -0.3125 to 0.3125
- output_bias: float32 [384], replicated, may hold values from -3 to 3
Outputs:
- encoded: bfloat16 [4, 8, 4, 32, 384], P('clips', 'tm', 'rows'), parts along dimension 0
There are 2 independent parts, one for each index of `clips`. A program takes and returns all parts, laid end to end along the dimension named above; an argument that names none is the same for every part. Nothing has to cross between parts.
Inputs may be any that keep to these rules, and one draw needn't show every extreme that they name: The valid frames of a clip in a section are that section's first lengths[b, s] frame slots.
All inputs are finite; a program needn't handle non-finite values.
Results may differ from a plain program's by a relative error of at most 0.0062.
Values may be sent and summed in bfloat16 or wider, within the bound.
No kernel may reach another device: no remote copies, remote signals or barrier semaphores. Data moves between devices by JAX's collectives and lax.ppermute only.
A program may use at most 128 MiB of HBM per device.

v0:
```python
import math
import jax
import jax.numpy as jnp
from jax import lax
from jax.sharding import PartitionSpec as P

EPSILON = 1e-06


def prefix(part, axis, combine, identity):
    place = lax.axis_index(axis)
    gathered = jax.tree.map(lambda a: lax.all_gather(a, axis), part)
    state = jax.tree.map(lambda a, e: jnp.zeros_like(a) + jnp.asarray(e, a.dtype), part, identity)

    def one(step, state):
        return combine(
            state, jax.tree.map(lambda a: lax.dynamic_index_in_dim(a, step, 0, False), gathered)
        )

    return lax.fori_loop(0, place, one, state)


def as_sent(x):

    def short(part):
        return part.astype(jnp.bfloat16) if part.dtype == jnp.float32 else part

    return jax.tree.map(short, x)


def with_halo(cells, sides, width):
    for axis, dim in sides:
        count = lax.axis_size(axis)
        ends = count - 1
        head = lax.slice_in_dim(cells, 0, width, axis=dim)
        tail = lax.slice_in_dim(cells, cells.shape[dim] - width, cells.shape[dim], axis=dim)
        cells = jnp.concatenate(
            [
                lax.ppermute(tail, axis, [(i, (i + 1) % count) for i in range(ends)]),
                cells,
                lax.ppermute(head, axis, [((i + 1) % count, i) for i in range(ends)]),
            ],
            axis=dim,
        )
    return cells


def normalize(field, gain):
    widened = field.astype(jnp.float32)
    return widened * lax.rsqrt(jnp.mean(widened * widened, axis=-1, keepdims=True) + EPSILON) * gain


def last_two(extended, counts):
    slot_total = extended.shape[1]
    chosen = []
    for position in range(2):
        target = counts + position
        picked = jnp.zeros_like(extended[:, 0])
        for slot_index in range(slot_total):
            matches = (target == slot_index)[:, None, None, None]
            picked = jnp.where(matches, extended[:, slot_index], picked)
        chosen.append(picked)
    return jnp.stack(chosen, axis=1)


def summarize(activated, counts):
    blanks = jnp.zeros((activated.shape[0], 2) + activated.shape[2:], activated.dtype)
    summary = last_two(jnp.concatenate([blanks, activated], axis=1), counts)
    return (summary, jnp.minimum(counts, 2).astype(jnp.bfloat16))


def join_later(earlier, later):
    early_frames, early_count = earlier
    late_frames, late_count = later
    complete = (late_count > 1.5)[:, None, None, None, None]
    single = (late_count > 0.5)[:, None, None, None, None]
    shifted = jnp.concatenate([early_frames[:, 1:], late_frames[:, 1:]], axis=1)
    frames = jnp.where(complete, late_frames, jnp.where(single, shifted, early_frames))
    total_count = jnp.minimum(early_count + late_count, 2.0).astype(early_count.dtype)
    return (frames, total_count)


def incoming_cache(summary, counts):
    starting = (jnp.zeros_like(summary), jnp.zeros_like(counts))
    combined = prefix((summary, counts), "tm", join_later, starting)
    return combined[0]


def convolve(padded, causal_weight, causal_bias):
    clip_count, slot_total, rows_padded, column_count, channels = padded.shape
    frame_count = slot_total - 2
    row_count = rows_padded - 2
    widened = jnp.pad(padded, ((0, 0), (0, 0), (0, 0), (1, 1), (0, 0)))
    summed = jnp.zeros((clip_count * frame_count * row_count * column_count, channels), jnp.float32)
    for delta_time in range(3):
        for delta_row in range(3):
            window = widened[
                :, delta_time : delta_time + frame_count, delta_row : delta_row + row_count
            ]
            columns = jnp.concatenate(
                [window[:, :, :, delta_col : delta_col + column_count] for delta_col in range(3)],
                axis=-1,
            )
            kernel = causal_weight[delta_time, delta_row].reshape(3 * channels, channels)
            summed = summed + jnp.dot(
                columns.reshape(-1, 3 * channels), kernel, preferred_element_type=jnp.float32
            )
    return summed.reshape(clip_count, frame_count, row_count, column_count, channels) + causal_bias


def attend(normed, triple_weight, triple_bias, output_weight, output_bias):
    frame_count, places, channels = normed.shape
    packed = (
        jnp.dot(normed.reshape(-1, channels), triple_weight, preferred_element_type=jnp.float32)
        + triple_bias
    )
    packed = packed.reshape(frame_count, places, 3 * channels)
    queries = packed[:, :, :channels]
    key_vectors = packed[:, :, channels : 2 * channels]
    values = packed[:, :, 2 * channels :].astype(jnp.bfloat16)
    scores = jnp.einsum(
        "nqc,nkc->nqk", queries, key_vectors, precision=lax.Precision.HIGHEST
    ) / math.sqrt(channels)
    row_max = jnp.max(scores, axis=-1, keepdims=True)
    exponent = jnp.exp(scores - row_max)
    weights = (exponent / jnp.sum(exponent, axis=-1, keepdims=True)).astype(jnp.bfloat16)
    attended = jnp.einsum(
        "nqk,nkc->nqc", weights, values, preferred_element_type=jnp.float32
    ).astype(jnp.bfloat16)
    projected = (
        jnp.dot(attended.reshape(-1, channels), output_weight, preferred_element_type=jnp.float32)
        + output_bias
    )
    return projected.reshape(frame_count, places, channels).astype(jnp.bfloat16)


def body(
    segment_input,
    inner_input,
    lengths,
    inner_gain,
    causal_weight,
    causal_bias,
    attention_gain,
    triple_weight,
    triple_bias,
    output_weight,
    output_bias,
):
    clip_count, frame_count, row_count, column_count, channels = segment_input.shape
    activated = jax.nn.silu(normalize(inner_input, inner_gain)).astype(jnp.bfloat16)
    counts = lengths[:, 0]
    live_mask = (jnp.arange(frame_count, dtype=jnp.int32)[None, :] < counts[:, None]).astype(
        jnp.float32
    )
    carried = incoming_cache(*summarize(activated, counts))
    extended = jnp.concatenate([carried, activated], axis=1)
    padded = with_halo(as_sent(extended), (("rows", 2),), 1).astype(extended.dtype)
    convolved = convolve(padded, causal_weight, causal_bias)
    residual = (segment_input.astype(jnp.float32) + convolved).astype(jnp.bfloat16)
    residual = lax.optimization_barrier(residual)
    normed = normalize(residual, attention_gain).astype(jnp.bfloat16)
    row_devices = lax.axis_size("rows")
    per_device = clip_count * frame_count // row_devices
    grouped = normed.reshape(row_devices, per_device, row_count, column_count, channels)
    portion = lax.all_to_all(grouped, "rows", split_axis=0, concat_axis=2, tiled=True)
    owned = portion.shape[1]
    height = portion.shape[2]
    flat = portion.reshape(owned, height * column_count, channels)
    result = attend(flat, triple_weight, triple_bias, output_weight, output_bias)
    result = result.reshape(1, owned, height, column_count, channels)
    projected = lax.all_to_all(result, "rows", split_axis=2, concat_axis=0, tiled=True)
    projected = projected.reshape(clip_count, frame_count, row_count, column_count, channels)
    projected = lax.optimization_barrier(projected)
    summed = residual.astype(jnp.float32) + projected.astype(jnp.float32)
    return (summed * live_mask[:, :, None, None, None]).astype(jnp.bfloat16)


def activate(field, gain):
    return jax.nn.silu(normalize(field, gain)).astype(jnp.bfloat16)


def conv3d(frames, causal_weight, time_padding):
    return lax.conv_general_dilated(
        frames,
        causal_weight,
        window_strides=(1, 1, 1),
        padding=(time_padding, (1, 1), (1, 1)),
        dimension_numbers=("NDHWC", "DHWIO", "NDHWC"),
        preferred_element_type=jnp.float32,
    )


def gathered_body(
    segment_input,
    inner_input,
    lengths,
    inner_gain,
    causal_weight,
    causal_bias,
    attention_gain,
    triple_weight,
    triple_bias,
    output_weight,
    output_bias,
):
    clip_count, frame_count, row_count, column_count, channels = segment_input.shape
    sections = lax.axis_size("tm")
    counts = lengths[:, 0]
    ahead = [(i, i + 1) for i in range(sections - 1)]
    prev_counts = lax.ppermute(counts, "tm", ahead)
    both = jnp.concatenate([inner_input, segment_input], axis=0)
    both_all = lax.all_gather(both, "rows", axis=2, tiled=True)
    inner_all = both_all[:clip_count]
    segment_all = both_all[clip_count:]
    wide = (counts > 1)[:, None, None, None]
    last_raw = jnp.where(wide, inner_all[:, frame_count - 1], inner_all[:, 0])
    prev_raw = lax.ppermute(inner_all, "tm", ahead)
    before_raw = lax.ppermute(last_raw, "tm", [(i, i + 2) for i in range(sections - 2)])
    own = activate(inner_all, inner_gain)
    own_part = conv3d(own, causal_weight, (2, 0))
    prev = activate(prev_raw, inner_gain)
    before = activate(before_raw, inner_gain)
    prev_wide = (prev_counts > 1)[:, None, None, None]
    carried = jnp.stack(
        [
            jnp.where(prev_wide, prev[:, frame_count - 2], before),
            jnp.where(prev_wide, prev[:, frame_count - 1], prev[:, 0]),
        ],
        axis=1,
    )
    carried_part = conv3d(carried, causal_weight, (0, frame_count))
    convolved = own_part + carried_part + causal_bias
    residual = (segment_all.astype(jnp.float32) + convolved).astype(jnp.bfloat16)
    normed = normalize(residual, attention_gain).astype(jnp.bfloat16)
    height = normed.shape[2]
    frames = clip_count * frame_count
    places = height * column_count
    flat = normed.reshape(frames * places, channels)
    packed = (
        jnp.dot(flat, triple_weight[:, channels:], preferred_element_type=jnp.float32)
        + triple_bias[channels:]
    ).reshape(frames, places, 2 * channels)
    key_vectors = packed[:, :, :channels]
    values = packed[:, :, channels:].astype(jnp.bfloat16)
    start = lax.axis_index("rows") * row_count
    mine = lax.dynamic_slice_in_dim(normed, start, row_count, axis=2)
    queries = (
        jnp.dot(
            mine.reshape(-1, channels),
            triple_weight[:, :channels],
            preferred_element_type=jnp.float32,
        )
        + triple_bias[:channels]
    ).reshape(frames, row_count * column_count, channels)
    scores = jnp.einsum(
        "nqc,nkc->nqk", queries, key_vectors, precision=lax.Precision.HIGHEST
    ) / math.sqrt(channels)
    row_max = jnp.max(scores, axis=-1, keepdims=True)
    exponent = jnp.exp(scores - row_max)
    weights = (exponent / jnp.sum(exponent, axis=-1, keepdims=True)).astype(jnp.bfloat16)
    attended = jnp.einsum(
        "nqk,nkc->nqc", weights, values, preferred_element_type=jnp.float32
    ).astype(jnp.bfloat16)
    projected = (
        jnp.dot(attended.reshape(-1, channels), output_weight, preferred_element_type=jnp.float32)
        + output_bias
    ).astype(jnp.bfloat16)
    projected = projected.reshape(clip_count, frame_count, row_count, column_count, channels)
    residual_mine = lax.dynamic_slice_in_dim(residual, start, row_count, axis=2)
    live_mask = (jnp.arange(frame_count, dtype=jnp.int32)[None, :] < counts[:, None]).astype(
        jnp.float32
    )
    summed = residual_mine.astype(jnp.float32) + projected.astype(jnp.float32)
    return (summed * live_mask[:, :, None, None, None]).astype(jnp.bfloat16)


GATHER_LIMIT = 1 << 22


def chosen_body(segment_input, inner_input, *rest):
    gathered = inner_input.size * inner_input.dtype.itemsize * lax.axis_size("rows")
    if gathered <= GATHER_LIMIT:
        return gathered_body(segment_input, inner_input, *rest)
    return body(segment_input, inner_input, *rest)


def solution(mesh):
    placed = (
        P("clips", "tm", "rows", None, None),
        P("clips", "tm", "rows", None, None),
        P("clips", "tm"),
        P(),
        P(),
        P(),
        P(),
        P(),
        P(),
        P(),
        P(),
    )
    return jax.shard_map(
        chosen_body,
        mesh=mesh,
        in_specs=placed,
        out_specs=P("clips", "tm", "rows", None, None),
        check_vma=False,
    )
```

profile of v0, /device:TPU:1, one launch (start us, length us, event | category | flops | bytes accessed | tf_op | source)
XLA Modules:
  0.0 64.8 jit_solution(6598093223761162605)
XLA Ops:
  0.0 4.6 %collective-permute-start = (s32[2]{0:T(128)}, s32[2]{0:T(128)S(1)}, u32[]{:S(2)}, u32[]{:S(2)}) collective-permute-start(s32[2]{0:T(128)} %bitcast.72), channel_id=1, source_target_pairs={{0,4},{4,8},{8,12},{1,5},{5,9},{9,13},{2,6},{6,10},{10,14},{3,7},{... | collective-permute-start | bytes 32 | tf_op jit(solution)/shard_map/ppermute | solution.py:211
  4.6 0.7 %broadcast_compare_fusion = pred[2]{0:T(512)(128)(4,1)S(1)} fusion(s32[2,1]{0,1:T(1,128)} %param.13), kind=kLoop, calls=%fused_computation.89 | loop fusion | flops 2 | bytes 10 | tf_op jit(solution)/shard_map/gt | solution.py:216
  5.3 1.0 %pad_maximum_fusion = bf16[4,2,1,32,384]{4,3,1,0,2:T(8,128)(2,1)S(1)} fusion(bf16[2,2,1,32,384]{4,3,1,0,2:T(8,128)(2,1)} %bitcast.70, bf16[2,2,1,32,384]{4,3,1,0,2:T(8,128)(2,1)} %bitcast.71), kind=kLoop, calls=%fused_computation.71 | loop fusion | flops 98304 | bytes 393216 | tf_op jit(solution)/shard_map/concatenate | solution.py:212
  6.3 17.9 %all_gather.3 = bf16[4,2,4,32,384]{4,3,1,0,2:T(8,128)(2,1)S(1)} all-gather(bf16[4,2,1,32,384]{4,3,1,0,2:T(8,128)(2,1)S(1)} %pad_maximum_fusion), channel_id=1, replica_groups=mesh['clips'=2,'tm'=4,'rows'=4] {'rows'}, dimensions={2}, use_global_device_ids=true | all-gather | bytes 983040 | tf_op jit(solution)/shard_map/all_gather | solution.py:213
  24.3 1.3 %collective-permute-start.2 = (bf16[2,4,32,384]{3,2,0,1:T(8,128)(2,1)S(1)}, bf16[2,4,32,384]{3,2,0,1:T(8,128)(2,1)S(1)}, u32[]{:S(2)}, u32[]{:S(2)}) collective-permute-start(bf16[2,4,32,384]{3,2,0,1:T(8,128)(2,1)S(1)} %fusion.48), channel_id=1, source_target_pairs={{0,8},{4,12},{1,9},{5,13},{2,10},{6,14},{3,11},{7,15},{16,24},{20,... | collective-permute-start | bytes 589832 | tf_op jit(solution)/shard_map/ppermute | solution.py:219
  25.8 3.9 %collective-permute-start.1 = (bf16[2,2,4,32,384]{4,3,0,2,1:T(8,128)(2,1)S(1)}, bf16[2,2,4,32,384]{4,3,0,2,1:T(8,128)(2,1)S(1)}, u32[]{:S(2)}, u32[]{:S(2)}) collective-permute-start(bf16[2,2,4,32,384]{4,3,0,2,1:T(8,128)(2,1)S(1)} %copy.107), channel_id=1, source_target_pairs={{0,4},{4,8},{8,12},{1,5},{5,9},{9,13},{2,6},{6,10},{10,14},{3,7},{... | collective-permute-start | bytes 1179656 | tf_op jit(solution)/shard_map/ppermute | solution.py:218
  29.8 0.2 fusion.8
  30.1 5.5 %collective-permute-done.1 = bf16[2,2,4,32,384]{4,3,0,2,1:T(8,128)(2,1)S(1)} collective-permute-done((bf16[2,2,4,32,384]{4,3,0,2,1:T(8,128)(2,1)S(1)}, bf16[2,2,4,32,384]{4,3,0,2,1:T(8,128)(2,1)S(1)}, u32[]{:S(2)}, u32[]{:S(2)}) %collective-permute-start.1) | collective-permute-done | bytes 393248 | tf_op jit(solution)/shard_map/ppermute | solution.py:218
  35.6 0.2 fusion.16
  35.8 0.5 fusion.45
  36.3 0.3 copy.110
  36.7 0.4 pad.clone
  37.0 0.1 slice.57
  37.1 0.6 fusion.30
  37.8 0.2 fusion.51
  38.1 0.3 copy.111
  38.5 0.4 pad.2.clone
  39.0 0.6 fusion.31
  39.6 13.2 %convolution_select_fusion = f32[2,4,16,5,384]{4,2,3,1,0:T(8,128)S(1)} fusion(bf16[3,3,3,384,384]{4,3,2,1,0:T(8,128)(2,1)} %param.15, bf16[2,4,2,8,7,384]{5,2,4,3,1,0:T(2,128)(2,1)S(1)} %fusion.31, pred[16,5]{0,1:T(8,128)(4,1)S(1)} %copy-done.4), kind=kOutput, calls=%fused_computation.5 | convolution fusion | flops 2123612160 | bytes 9633872 | tf_op jit(solution)/shard_map/conv_general_dilated | solution.py:184
  52.8 7.0 %fusion.4 = f32[2,4,16,5,384]{4,2,3,1,0:T(8,128)S(1)} fusion(f32[2,4,16,5,384]{4,2,3,1,0:T(8,128)S(1)} %convolution_select_fusion, bf16[3,3,3,384,384]{4,3,2,1,0:T(8,128)(2,1)S(1)} %bitcast.57, bf16[2,4,2,8,7,384]{5,2,4,3,1,0:T(2,128)(2,1)S(1)} %fusion.30, f32[384]{0:T(512)S(1)} %copy-done.5, pred[16,5]{0,1:T(8,128)(4,1)S(1)} %copy-done.4), kind=kOutput, calls=%fused_computation.8 | convolution fusion | flops 2124103680 | bytes 10618448 | tf_op jit(solution)/shard_map/conv_general_dilated | solution.py:184
  59.9 0.4 copy.101
  60.4 0.2 fusion.24
  60.6 0.3 copy-done.6
  60.9 0.2 fusion.26
  61.1 0.4 copy-done.1
  61.5 0.2 convolution_add_fusion.2
  61.7 0.6 convolution_add_fusion
  62.3 0.9 %convolution_multiply_fusion = f32[4,32,128]{2,1,0:T(8,128)S(1)} fusion(f32[4,32,384]{2,1,0:T(8,128)S(1)} %bitcast.66, f32[4,128,768]{2,1,0:T(8,128)S(1)} %bitcast.58), kind=kOutput, calls=%fused_computation.15 | convolution fusion | flops 75513856 | bytes 1048576 | tf_op jit(solution)/shard_map/nqc,nkc->nqk/dot_general | solution.py:256
  63.3 0.2 fusion.60
  63.5 0.3 convolution_convert_fusion
  63.8 0.2 fusion.5
  64.0 0.7 %fusion.50 = bf16[2,2,1,32,384]{4,3,2,1,0:T(8,128)(2,1)} fusion(bf16[2,2,1,32,384]{4,3,2,1,0:T(8,128)(2,1)S(1)} %bitcast.69, f32[2,2]{1,0:T(2,128)S(1)} %compare_convert_fusion, bf16[2,2,4,32,384]{4,3,2,1,0:T(8,128)(2,1)S(1)} %get-tuple-element.6, s32[]{:T(128)S(6)} %select_n.18), kind=kLoop, calls=%fused_computation.74 | loop fusion | flops 245760 | bytes 294932 | tf_op jit(solution)/shard_map/convert_element_type | solution.py:275
  (43 shorter events, 1.0 us)
Async XLA Ops:
  0.0 63.8 %copy-start = (bf16[384,384]{1,0:T(8,128)(2,1)S(1)}, bf16[384,384]{1,0:T(8,128)(2,1)}, u32[]{:S(2)}) copy-start(bf16[384,384]{1,0:T(8,128)(2,1)} %param.20) | copy-start | bytes 884740
  0.0 30.0 %collective-permute-start = (s32[2]{0:T(128)}, s32[2]{0:T(128)S(1)}, u32[]{:S(2)}, u32[]{:S(2)}) collective-permute-start(s32[2]{0:T(128)} %bitcast.72), channel_id=1, source_target_pairs={{0,4},{4,8},{8,12},{1,5},{5,9},{9,13},{2,6},{6,10},{10,14},{3,7},{... | collective-permute-start | bytes 32 | tf_op jit(solution)/shard_map/ppermute | solution.py:211
  24.2 5.5 %copy-start.8 = (s32[2,1]{0,1:T(1,128)S(1)}, s32[2,1]{0,1:T(1,128)}, u32[]{:S(2)}) copy-start(s32[2,1]{0,1:T(1,128)} %param.13) | copy-start | bytes 28
  24.2 5.6 %copy-start.3 = (f32[1152]{0:T(1024)S(1)}, f32[1152]{0:T(1024)}, u32[]{:S(2)}) copy-start(f32[1152]{0:T(1024)} %param.19) | copy-start | bytes 13828
  24.3 11.5 %copy-start.2 = (f32[384]{0:T(512)S(1)}, f32[384]{0:T(512)}, u32[]{:S(2)}) copy-start(f32[384]{0:T(512)} %param.14) | copy-start | bytes 4612
  24.3 5.7 %collective-permute-start.2 = (bf16[2,4,32,384]{3,2,0,1:T(8,128)(2,1)S(1)}, bf16[2,4,32,384]{3,2,0,1:T(8,128)(2,1)S(1)}, u32[]{:S(2)}, u32[]{:S(2)}) collective-permute-start(bf16[2,4,32,384]{3,2,0,1:T(8,128)(2,1)S(1)} %fusion.48), channel_id=1, source_target_pairs={{0,8},{4,12},{1,9},{5,13},{2,10},{6,14},{3,11},{7,15},{16,24},{20,... | collective-permute-start | bytes 589832 | tf_op jit(solution)/shard_map/ppermute | solution.py:219
  25.8 9.8 %collective-permute-start.1 = (bf16[2,2,4,32,384]{4,3,0,2,1:T(8,128)(2,1)S(1)}, bf16[2,2,4,32,384]{4,3,0,2,1:T(8,128)(2,1)S(1)}, u32[]{:S(2)}, u32[]{:S(2)}) collective-permute-start(bf16[2,2,4,32,384]{4,3,0,2,1:T(8,128)(2,1)S(1)} %copy.107), channel_id=1, source_target_pairs={{0,4},{4,8},{8,12},{1,5},{5,9},{9,13},{2,6},{6,10},{10,14},{3,7},{... | collective-permute-start | bytes 1179656 | tf_op jit(solution)/shard_map/ppermute | solution.py:218
  38.1 1.4 %copy-start.4 = (pred[16,5]{0,1:T(8,128)(4,1)S(1)}, pred[16,5]{0,1:T(8,128)(4,1)}, u32[]{:S(2)}) copy-start(pred[16,5]{0,1:T(8,128)(4,1)} %constant.44) | copy-start | bytes 244
  39.0 13.8 %slice-start = ((s8[7962624]{0:T(1024)(128)(4,1)}), s8[4194304]{0:T(1024)(128)(4,1)S(1)}, s32[]{:S(2)}) async-start(s8[7962624]{0:T(1024)(128)(4,1)} %bitcast.56), calls=%async_computation | async-start | bytes 8388608
  39.6 13.2 %slice-start.1 = ((s8[7962624]{0:T(1024)(128)(4,1)}), s8[3768320]{0:T(1024)(128)(4,1)S(1)}, s32[]{:S(2)}) async-start(s8[7962624]{0:T(1024)(128)(4,1)} %bitcast.56), calls=%async_computation.1 | async-start | bytes 7536640
  39.6 13.2 %copy-start.5 = (f32[384]{0:T(512)S(1)}, f32[384]{0:T(512)}, u32[]{:S(2)}) copy-start(f32[384]{0:T(512)} %param.16) | copy-start | bytes 4612
  60.2 0.7 %copy-start.6 = (f32[384]{0:T(512)S(1)}, f32[384]{0:T(512)}, u32[]{:S(2)}) copy-start(f32[384]{0:T(512)} %param.17) | copy-start | bytes 4612
  60.3 1.2 %copy-start.1 = (bf16[384,1152]{1,0:T(8,128)(2,1)S(1)}, bf16[384,1152]{1,0:T(8,128)(2,1)}, u32[]{:S(2)}) copy-start(bf16[384,1152]{1,0:T(8,128)(2,1)} %param.18) | copy-start | bytes 2654212
  60.4 1.2 %slice-start.2 = ((f32[1152]{0:T(1024)}), f32[384]{0:T(512)S(1)}, s32[]{:S(2)}) async-start(f32[1152]{0:T(1024)} %param.19), calls=%async_computation.2 | async-start | bytes 4096 | tf_op jit(solution)/shard_map/slice | solution.py:254
  62.3 1.5 %copy-start.7 = (f32[384]{0:T(512)S(1)}, f32[384]{0:T(512)}, u32[]{:S(2)}) copy-start(f32[384]{0:T(512)} %param.21) | copy-start | bytes 4612
where the time goes:
time: 65 us; the launch traced here: 64.8 us
  matrix products  22.4 us (34%)
  blocking collectives  17.9 us (28%)
  starting transfers between devices  9.81 us (15%)
  other arithmetic  5.62 us (9%)
  waiting for transfers between devices  5.46 us (8%)
  local copies, waits for them, and re-layouts  3.06 us (5%)
    conv_general_dilated x2, matrix products, conv3d(): lax.conv_general_dilated(frames, causal_weight, window_strides=(1, 1, 1),...  20.2 us
    all_gather x1, blocking collectives, gathered_body(): both_all = lax.all_gather(both, 'rows', axis=2, tiled=True)  17.9 us
    ppermute x1, waiting for transfers between devices, gathered_body(): prev_raw = lax.ppermute(inner_all, 'tm', ahead)  5.46 us
    ppermute x1, starting transfers between devices, gathered_body(): prev_counts = lax.ppermute(counts, 'tm', ahead)  4.63 us
    ppermute x1, starting transfers between devices, gathered_body(): prev_raw = lax.ppermute(inner_all, 'tm', ahead)  3.88 us
    unnamed x25, local copies, waits for them, and re-layouts  1.5 us
    ppermute x1, starting transfers between devices, gathered_body(): lax.ppermute(last_raw, 'tm', [(i, i + 2) for i in range(sections - 2)])  1.3 us
  transfers between devices with their start and end apart: 3, of which 1 were waited for; matrix products, arithmetic and copies ran while one was open for 3% of the time, Pallas kernels for 0%

commit v1 on v0

--- a/solution.py
+++ b/solution.py
@@ -210,7 +210,20 @@
     ahead = [(i, i + 1) for i in range(sections - 1)]
     prev_counts = lax.ppermute(counts, "tm", ahead)
     both = jnp.concatenate([inner_input, segment_input], axis=0)
-    both_all = lax.all_gather(both, "rows", axis=2, tiled=True)
+    inbox = []
+    extent = jax.lax.axis_size("rows")
+    for i0 in tuple(range(extent)):
+        inbox.append((i0, (i0 + 1) % extent))
+    in_order = []
+    for i0 in tuple(range(extent)):
+        in_order.append((i0, (i0 - 1) % extent))
+    part_next, even = ([both], [both])
+    for _ in range(extent // 2):
+        part_next.append(jax.lax.ppermute(part_next[-1], "rows", inbox))
+    for _ in [*range((extent - 1) // 2)]:
+        even.append(jax.lax.ppermute(even[-1], "rows", in_order))
+    formed = jnp.concatenate([*part_next[::-1], *even[1:]], 2)
+    both_all = jnp.roll(formed, (jax.lax.axis_index("rows") - extent // 2) * both.shape[2], 2)
     inner_all = both_all[:clip_count]
     segment_all = both_all[clip_count:]
     wide = (counts > 1)[:, None, None, None]

time: 65 us -> 59 us (0.908)
  blocking collectives: 17.9 us -> 0 us
  waiting for transfers between devices: 5.46 us -> 13.8 us
  matrix products: 22.4 us -> 16.5 us
  starting transfers between devices: 9.81 us -> 14.8 us
  local copies, waits for them, and re-layouts: 3.06 us -> 7.76 us
    all_gather x1 -> x0, blocking collectives: 17.9 us -> none  [gathered_body(): both_all = lax.all_gather(both, 'rows', axis=2, tiled=True)]
    ppermute x1, waiting for transfers between devices: 0.01 us -> 7.49 us  [gathered_body(): lax.ppermute(last_raw, 'tm', [(i, i + 2) for i in range(sections - 2)])]
    ppermute x0 -> x3, waiting for transfers between devices: none -> 6.3 us  [the longest x2 6.29 us: gathered_body(): part_next.append(jax.lax.ppermute(part_next[-1], 'rows', inbox))]
    conv_general_dilated x2, matrix products: 20.2 us -> 14.2 us  [conv3d(): lax.conv_general_dilated(frames, causal_weight, window_strides=(1, 1, 1),...]
    ppermute x1, waiting for transfers between devices: 5.46 us -> 0.01 us  [gathered_body(): prev_raw = lax.ppermute(inner_all, 'tm', ahead)]
    ppermute x0 -> x3, starting transfers between devices: none -> 4.27 us  [the longest x2 2.18 us: gathered_body(): part_next.append(jax.lax.ppermute(part_next[-1], 'rows', inbox))]
    unnamed x25 -> x35, local copies, waits for them, and re-layouts: 1.5 us -> 4.63 us
    ppermute x1, starting transfers between devices: 3.88 us -> 5.15 us  [gathered_body(): prev_raw = lax.ppermute(inner_all, 'tm', ahead)]
  transfers between devices with their start and end apart: 3 -> 6, of which waited for: 1 -> 2; matrix products, arithmetic and copies ran while one was open for 3% -> 7% of each run, Pallas kernels for 0% -> 0%
where the time goes in v1:
time: 59 us; the launch traced here: 58.7 us
  matrix products  16.5 us (28%)
  starting transfers between devices  14.8 us (25%)
  waiting for transfers between devices  13.8 us (23%)
  local copies, waits for them, and re-layouts  7.76 us (13%)
  other arithmetic  5.32 us (9%)
    conv_general_dilated x2, matrix products, conv3d(): lax.conv_general_dilated(frames, causal_weight, window_strides=(1, 1, 1),...  14.2 us
    ppermute x1, waiting for transfers between devices, gathered_body(): lax.ppermute(last_raw, 'tm', [(i, i + 2) for i in range(sections - 2)])  7.49 us
    ppermute x2, waiting for transfers between devices, gathered_body(): part_next.append(jax.lax.ppermute(part_next[-1], 'rows', inbox))  6.29 us
    ppermute x1, starting transfers between devices, gathered_body(): prev_raw = lax.ppermute(inner_all, 'tm', ahead)  5.15 us
    unnamed x35, local copies, waits for them, and re-layouts  4.63 us
    ppermute x1, starting transfers between devices, gathered_body(): prev_counts = lax.ppermute(counts, 'tm', ahead)  4.11 us
    ppermute x2, starting transfers between devices, gathered_body(): part_next.append(jax.lax.ppermute(part_next[-1], 'rows', inbox))  2.18 us
    ppermute x1, starting transfers between devices, gathered_body(): even.append(jax.lax.ppermute(even[-1], 'rows', in_order))  2.09 us
  transfers between devices with their start and end apart: 6, of which 2 were waited for; matrix products, arithmetic and copies ran while one was open for 7% of the time, Pallas kernels for 0%

profile of v1, /device:TPU:1, one launch (start us, length us, event | category | flops | bytes accessed | tf_op | source)
XLA Modules:
  0.0 58.7 jit_solution(10241180790332955674)
XLA Ops:
  0.0 1.0 %constant_dynamic-update-slice_fusion.1 = bf16[4,2,1,32,384]{4,3,2,1,0:T(8,128)(2,1)S(1)} fusion(bf16[2,2,1,32,384]{4,3,2,1,0:T(8,128)(2,1)} %param.12), kind=kLoop, calls=%fused_computation.78 | loop fusion | bytes 196608
  1.0 0.9 %constant_dynamic-update-slice_fusion = bf16[4,2,1,32,384]{4,3,2,1,0:T(8,128)(2,1)S(1)} fusion(bf16[4,2,1,32,384]{4,3,2,1,0:T(8,128)(2,1)S(1)} %constant_dynamic-update-slice_fusion.1, bf16[2,2,1,32,384]{4,3,2,1,0:T(8,128)(2,1)} %param.11), kind=kLoop, calls=%fused_computation.77 | loop fusion | bytes 196608 | tf_op jit(solution)/shard_map/concatenate | solution.py:212
  1.9 2.2 %collective-permute-start = (bf16[4,2,1,32,384]{4,3,2,1,0:T(8,128)(2,1)S(1)}, bf16[4,2,1,32,384]{4,3,2,1,0:T(8,128)(2,1)S(1)}, u32[]{:S(2)}, u32[]{:S(2)}) collective-permute-start(bf16[4,2,1,32,384]{4,3,2,1,0:T(8,128)(2,1)S(1)} %constant_dynamic-update-slice_fusion), channel_id=1, source_target_pairs={{0,1},{1,2},{2,3},{3,0},{4,5},{5,6},{6,7},{7,4},{8,9},{9,10},{10,1... | collective-permute-start | bytes 589832 | tf_op jit(solution)/shard_map/ppermute | solution.py:222
  4.1 2.1 %collective-permute-start.2 = (bf16[4,2,1,32,384]{4,3,2,1,0:T(8,128)(2,1)S(1)}, bf16[4,2,1,32,384]{4,3,2,1,0:T(8,128)(2,1)S(1)}, u32[]{:S(2)}, u32[]{:S(2)}) collective-permute-start(bf16[4,2,1,32,384]{4,3,2,1,0:T(8,128)(2,1)S(1)} %constant_dynamic-update-slice_fusion), channel_id=1, source_target_pairs={{0,3},{1,0},{2,1},{3,2},{4,7},{5,4},{6,5},{7,6},{8,11},{9,8},{10,9... | collective-permute-start | bytes 589832 | tf_op jit(solution)/shard_map/ppermute | solution.py:224
  6.2 4.1 %collective-permute-start.3 = (s32[2]{0:T(128)}, s32[2]{0:T(128)S(1)}, u32[]{:S(2)}, u32[]{:S(2)}) collective-permute-start(s32[2]{0:T(128)} %bitcast.68), channel_id=1, source_target_pairs={{0,4},{4,8},{8,12},{1,5},{5,9},{9,13},{2,6},{6,10},{10,14},{3,7},{... | collective-permute-start | bytes 32 | tf_op jit(solution)/shard_map/ppermute | solution.py:211
  10.3 0.7 %slice.49 = f32[768]{0:T(1024)S(1)} slice(f32[1152]{0:T(1024)} %param.19), slice={[384:1152]} | slice | bytes 6144 | tf_op jit(solution)/shard_map/slice | solution.py:255
  11.0 0.7 %compare_convert_fusion = f32[2,2]{1,0:T(2,128)S(1)} fusion(s32[2]{0:T(128)} %bitcast.69), kind=kLoop, calls=%fused_computation.95 | loop fusion | flops 8 | bytes 24 | tf_op jit(solution)/shard_map/convert_element_type | solution.py:284
  11.7 0.7 %broadcast_compare_fusion = pred[2]{0:T(512)(128)(4,1)S(1)} fusion(s32[2,1]{0,1:T(1,128)} %param.13), kind=kLoop, calls=%fused_computation.99 | loop fusion | flops 2 | bytes 10 | tf_op jit(solution)/shard_map/gt | solution.py:229
  12.4 6.3 %collective-permute-done.1 = bf16[4,2,1,32,384]{4,3,2,1,0:T(8,128)(2,1)S(1)} collective-permute-done((bf16[4,2,1,32,384]{4,3,2,1,0:T(8,128)(2,1)S(1)}, bf16[4,2,1,32,384]{4,3,2,1,0:T(8,128)(2,1)S(1)}, u32[]{:S(2)}, u32[]{:S(2)}) %collective-permute-start.1) | collective-permute-done | bytes 196640 | tf_op jit(solution)/shard_map/ppermute | solution.py:222
  18.8 0.9 %constant_dynamic-update-slice_fusion.9 = bf16[4,2,8,32,384]{4,3,2,1,0:T(8,128)(2,1)S(1)} fusion(bf16[4,2,8,32,384]{4,3,2,1,0:T(8,128)(2,1)S(1)} %constant_dynamic-update-slice_fusion.10, bf16[2,2,1,32,384]{4,3,2,1,0:T(8,128)(2,1)} %param.12), kind=kLoop, calls=%fused_computation.86 | loop fusion | bytes 196608
  19.7 0.9 %constant_dynamic-update-slice_fusion.8 = bf16[4,2,8,32,384]{4,3,2,1,0:T(8,128)(2,1)S(1)} fusion(bf16[4,2,8,32,384]{4,3,2,1,0:T(8,128)(2,1)S(1)} %constant_dynamic-update-slice_fusion.9, bf16[2,2,1,32,384]{4,3,2,1,0:T(8,128)(2,1)} %param.11), kind=kLoop, calls=%fused_computation.85 | loop fusion | bytes 196608
  21.1 5.2 %collective-permute-start.4 = (bf16[2,2,4,32,384]{4,3,2,0,1:T(8,128)(2,1)S(1)}, bf16[2,2,4,32,384]{4,3,2,0,1:T(8,128)(2,1)S(1)}, u32[]{:S(2)}, u32[]{:S(2)}) collective-permute-start(bf16[2,2,4,32,384]{4,3,2,0,1:T(8,128)(2,1)S(1)} %copy.70), channel_id=1, source_target_pairs={{0,4},{4,8},{8,12},{1,5},{5,9},{9,13},{2,6},{6,10},{10,14},{3,7},{... | collective-permute-start | bytes 1179656 | tf_op jit(solution)/shard_map/ppermute | solution.py:231
  26.4 1.3 %collective-permute-start.5 = (bf16[2,4,32,384]{3,2,1,0:T(8,128)(2,1)S(1)}, bf16[2,4,32,384]{3,2,1,0:T(8,128)(2,1)S(1)}, u32[]{:S(2)}, u32[]{:S(2)}) collective-permute-start(bf16[2,4,32,384]{3,2,1,0:T(8,128)(2,1)S(1)} %fusion.48), channel_id=1, source_target_pairs={{0,8},{4,12},{1,9},{5,13},{2,10},{6,14},{3,11},{7,15},{16,24},{20,... | collective-permute-start | bytes 589832 | tf_op jit(solution)/shard_map/ppermute | solution.py:232
  27.7 7.5 %collective-permute-done.5 = bf16[2,4,32,384]{3,2,1,0:T(8,128)(2,1)S(1)} collective-permute-done((bf16[2,4,32,384]{3,2,1,0:T(8,128)(2,1)S(1)}, bf16[2,4,32,384]{3,2,1,0:T(8,128)(2,1)S(1)}, u32[]{:S(2)}, u32[]{:S(2)}) %collective-permute-start.5) | collective-permute-done | bytes 196640 | tf_op jit(solution)/shard_map/ppermute | solution.py:232
  35.5 0.5 fusion.45
  36.2 0.2 fusion.51
  36.5 0.4 copy.74
  36.9 0.4 pad.2.clone
  37.4 0.6 fusion.31
  38.0 0.4 copy.73
  38.4 0.4 pad.clone
  38.9 0.6 fusion.30
  39.5 7.0 %convolution_select_fusion = f32[2,4,16,5,384]{4,2,3,1,0:T(8,128)S(1)} fusion(bf16[3,3,3,384,384]{4,3,2,1,0:T(8,128)(2,1)S(1)} %bitcast.55, bf16[2,4,2,8,7,384]{5,2,4,3,1,0:T(2,128)(2,1)S(1)} %fusion.31, pred[16,5]{0,1:T(8,128)(4,1)S(1)} %copy-done.5), kind=kOutput, calls=%fused_computation.5 | convolution fusion | flops 2123612160 | bytes 9633872 | tf_op jit(solution)/shard_map/conv_general_dilated | solution.py:184
  46.6 7.2 %fusion.4 = f32[2,4,16,5,384]{4,2,3,1,0:T(8,128)S(1)} fusion(f32[2,4,16,5,384]{4,2,3,1,0:T(8,128)S(1)} %convolution_select_fusion, bf16[3,3,3,384,384]{4,3,2,1,0:T(8,128)(2,1)S(1)} %bitcast.55, bf16[2,4,2,8,7,384]{5,2,4,3,1,0:T(2,128)(2,1)S(1)} %fusion.30, f32[384]{0:T(512)S(1)} %copy-done.6, pred[16,5]{0,1:T(8,128)(4,1)S(1)} %copy-done.5), kind=kOutput, calls=%fused_computation.8 | convolution fusion | flops 2124103680 | bytes 10618448 | tf_op jit(solution)/shard_map/conv_general_dilated | solution.py:184
  53.8 0.4 copy.66
  54.5 0.4 copy-done.7
  55.1 0.4 copy-done.1
  55.5 0.6 convolution_add_fusion
  56.1 0.2 convolution_add_fusion.2
  56.3 1.0 %convolution_multiply_fusion = f32[4,32,128]{2,1,0:T(8,128)S(1)} fusion(f32[4,32,384]{2,1,0:T(8,128)S(1)} %bitcast.64, f32[4,128,768]{2,1,0:T(8,128)S(1)} %bitcast.56), kind=kOutput, calls=%fused_computation.15 | convolution fusion | flops 75513856 | bytes 1048576 | tf_op jit(solution)/shard_map/nqc,nkc->nqk/dot_general | solution.py:269
  57.4 0.3 convolution_convert_fusion
  58.0 0.7 %fusion.50 = bf16[2,2,1,32,384]{4,3,2,1,0:T(8,128)(2,1)} fusion(bf16[2,2,1,32,384]{4,3,2,1,0:T(8,128)(2,1)S(1)} %bitcast.67, f32[2,2]{1,0:T(2,128)S(1)} %compare_convert_fusion, bf16[2,2,4,32,384]{4,3,2,1,0:T(8,128)(2,1)S(1)} %get-tuple-element.6, s32[]{:T(128)S(6)} %select_n.33), kind=kLoop, calls=%fused_computation.73 | loop fusion | flops 245760 | bytes 294932 | tf_op jit(solution)/shard_map/convert_element_type | solution.py:288
  (56 shorter events, 2.2 us)
Async XLA Ops:
  0.0 57.7 %copy-start = (bf16[384,384]{1,0:T(8,128)(2,1)S(1)}, bf16[384,384]{1,0:T(8,128)(2,1)}, u32[]{:S(2)}) copy-start(bf16[384,384]{1,0:T(8,128)(2,1)} %param.20) | copy-start | bytes 884740
  0.0 20.8 %copy-start.2 = (bf16[2,2,1,32,384]{4,3,2,1,0:T(8,128)(2,1)S(1)}, bf16[2,2,1,32,384]{4,3,2,1,0:T(8,128)(2,1)}, u32[]{:S(2)}) copy-start(bf16[2,2,1,32,384]{4,3,2,1,0:T(8,128)(2,1)} %param.12) | copy-start | bytes 294916
  0.0 20.8 %copy-start.3 = (bf16[2,2,1,32,384]{4,3,2,1,0:T(8,128)(2,1)S(1)}, bf16[2,2,1,32,384]{4,3,2,1,0:T(8,128)(2,1)}, u32[]{:S(2)}) copy-start(bf16[2,2,1,32,384]{4,3,2,1,0:T(8,128)(2,1)} %param.11) | copy-start | bytes 294916
  1.9 10.5 %collective-permute-start = (bf16[4,2,1,32,384]{4,3,2,1,0:T(8,128)(2,1)S(1)}, bf16[4,2,1,32,384]{4,3,2,1,0:T(8,128)(2,1)S(1)}, u32[]{:S(2)}, u32[]{:S(2)}) collective-permute-start(bf16[4,2,1,32,384]{4,3,2,1,0:T(8,128)(2,1)S(1)} %constant_dynamic-update-slice_fusion), channel_id=1, source_target_pairs={{0,1},{1,2},{2,3},{3,0},{4,5},{5,6},{6,7},{7,4},{8,9},{9,10},{10,1... | collective-permute-start | bytes 589832 | tf_op jit(solution)/shard_map/ppermute | solution.py:222
  4.1 16.5 %collective-permute-start.2 = (bf16[4,2,1,32,384]{4,3,2,1,0:T(8,128)(2,1)S(1)}, bf16[4,2,1,32,384]{4,3,2,1,0:T(8,128)(2,1)S(1)}, u32[]{:S(2)}, u32[]{:S(2)}) collective-permute-start(bf16[4,2,1,32,384]{4,3,2,1,0:T(8,128)(2,1)S(1)} %constant_dynamic-update-slice_fusion), channel_id=1, source_target_pairs={{0,3},{1,0},{2,1},{3,2},{4,7},{5,4},{6,5},{7,6},{8,11},{9,8},{10,9... | collective-permute-start | bytes 589832 | tf_op jit(solution)/shard_map/ppermute | solution.py:224
  6.2 6.2 %collective-permute-start.3 = (s32[2]{0:T(128)}, s32[2]{0:T(128)S(1)}, u32[]{:S(2)}, u32[]{:S(2)}) collective-permute-start(s32[2]{0:T(128)} %bitcast.68), channel_id=1, source_target_pairs={{0,4},{4,8},{8,12},{1,5},{5,9},{9,13},{2,6},{6,10},{10,14},{3,7},{... | collective-permute-start | bytes 32 | tf_op jit(solution)/shard_map/ppermute | solution.py:211
  12.4 6.3 %collective-permute-start.1 = (bf16[4,2,1,32,384]{4,3,2,1,0:T(8,128)(2,1)S(1)}, bf16[4,2,1,32,384]{4,3,2,1,0:T(8,128)(2,1)S(1)}, u32[]{:S(2)}, u32[]{:S(2)}) collective-permute-start(bf16[4,2,1,32,384]{4,3,2,1,0:T(8,128)(2,1)S(1)} %collective-permute-done), channel_id=1, source_target_pairs={{0,1},{1,2},{2,3},{3,0},{4,5},{5,6},{6,7},{7,4},{8,9},{9,10},{10,1... | collective-permute-start | bytes 589832 | tf_op jit(solution)/shard_map/ppermute | solution.py:222
  20.7 18.8 %slice-start = ((s8[7962624]{0:T(1024)(128)(4,1)}), s8[4194304]{0:T(1024)(128)(4,1)S(1)}, s32[]{:S(2)}) async-start(s8[7962624]{0:T(1024)(128)(4,1)} %bitcast.54), calls=%async_computation | async-start | bytes 8388608
  20.9 14.7 %copy-start.4 = (f32[384]{0:T(512)S(1)}, f32[384]{0:T(512)}, u32[]{:S(2)}) copy-start(f32[384]{0:T(512)} %param.14) | copy-start | bytes 4612
  21.1 14.2 %collective-permute-start.4 = (bf16[2,2,4,32,384]{4,3,2,0,1:T(8,128)(2,1)S(1)}, bf16[2,2,4,32,384]{4,3,2,0,1:T(8,128)(2,1)S(1)}, u32[]{:S(2)}, u32[]{:S(2)}) collective-permute-start(bf16[2,2,4,32,384]{4,3,2,0,1:T(8,128)(2,1)S(1)} %copy.70), channel_id=1, source_target_pairs={{0,4},{4,8},{8,12},{1,5},{5,9},{9,13},{2,6},{6,10},{10,14},{3,7},{... | collective-permute-start | bytes 1179656 | tf_op jit(solution)/shard_map/ppermute | solution.py:231
  26.4 8.8 %collective-permute-start.5 = (bf16[2,4,32,384]{3,2,1,0:T(8,128)(2,1)S(1)}, bf16[2,4,32,384]{3,2,1,0:T(8,128)(2,1)S(1)}, u32[]{:S(2)}, u32[]{:S(2)}) collective-permute-start(bf16[2,4,32,384]{3,2,1,0:T(8,128)(2,1)S(1)} %fusion.48), channel_id=1, source_target_pairs={{0,8},{4,12},{1,9},{5,13},{2,10},{6,14},{3,11},{7,15},{16,24},{20,... | collective-permute-start | bytes 589832 | tf_op jit(solution)/shard_map/ppermute | solution.py:232
  36.2 3.3 %slice-start.1 = ((s8[7962624]{0:T(1024)(128)(4,1)}), s8[3768320]{0:T(1024)(128)(4,1)S(1)}, s32[]{:S(2)}) async-start(s8[7962624]{0:T(1024)(128)(4,1)} %bitcast.54), calls=%async_computation.1 | async-start | bytes 7536640
  38.0 1.5 %copy-start.5 = (pred[16,5]{0,1:T(8,128)(4,1)S(1)}, pred[16,5]{0,1:T(8,128)(4,1)}, u32[]{:S(2)}) copy-start(pred[16,5]{0,1:T(8,128)(4,1)} %constant.67) | copy-start | bytes 244
  39.5 7.0 %copy-start.6 = (f32[384]{0:T(512)S(1)}, f32[384]{0:T(512)}, u32[]{:S(2)}) copy-start(f32[384]{0:T(512)} %param.16) | copy-start | bytes 4612
  54.2 0.7 %copy-start.7 = (f32[384]{0:T(512)S(1)}, f32[384]{0:T(512)}, u32[]{:S(2)}) copy-start(f32[384]{0:T(512)} %param.17) | copy-start | bytes 4612
  54.3 1.2 %copy-start.1 = (bf16[384,1152]{1,0:T(8,128)(2,1)S(1)}, bf16[384,1152]{1,0:T(8,128)(2,1)}, u32[]{:S(2)}) copy-start(bf16[384,1152]{1,0:T(8,128)(2,1)} %param.18) | copy-start | bytes 2654212
  55.1 1.0 %slice-start.2 = ((f32[1152]{0:T(1024)}), f32[384]{0:T(512)S(1)}, s32[]{:S(2)}) async-start(f32[1152]{0:T(1024)} %param.19), calls=%async_computation.2 | async-start | bytes 4096 | tf_op jit(solution)/shard_map/slice | solution.py:267
  56.0 1.7 %copy-start.8 = (f32[384]{0:T(512)S(1)}, f32[384]{0:T(512)}, u32[]{:S(2)}) copy-start(f32[384]{0:T(512)} %param.21) | copy-start | bytes 4612
